TPU v7x, 32 devices: a whole 2x2x4 slice. The times are simulated.
32 devices in a mesh: pole: 2 (over x), row: 8 (over z, y), col: 2 (over core).
Axes of the slice: x: 2, y: 2, z: 4, core: 2. Of those that a mesh axis runs over, the one named last changes fastest.
Arguments:
- anc_inverse: bfloat16 [2048, 1024], P(('pole', 'row')), parts along dimension 0, as said below
- parent_pivinv: float32 [2048, 1024], P(('pole', 'row')), parts along dimension 0, as said below
- parent_lower: bfloat16 [2048, 1024], P(('pole', 'row')), parts along dimension 0, may hold values from -0.1875 to 0.1875
- parent_mask: int32 [4], replicated, may hold values 0 or 1
- leaf_lower_par: bfloat16 [2048, 1024], P(('pole', 'row')), parts along dimension 0, may hold values from -0.125 to 0.125
- leaf_lower_anc: bfloat16 [2048, 1024], P(('pole', 'row')), parts along dimension 0, may hold values from -0.125 to 0.125
- leaf_mask: int32 [8], replicated, may hold values 0 or 1
- leaf_pivots: float32 [2048], P(('pole', 'col')), parts along dimension 0, may hold values from 0.5 to 2
Outputs:
- parent_block: float32 [2048, 1024], P(('pole', 'row')), parts along dimension 0
- parent_offdiag: bfloat16 [2048, 1024], P(('pole', 'row'), 'col'), parts along dimension 0
- leaf_par_block: bfloat16 [2048, 1024], P(('pole', 'row'), 'col'), parts along dimension 0
- leaf_anc_block: bfloat16 [2048, 1024], P(('pole', 'row'), 'col'), parts along dimension 0
- density: float32 [2048], P(('pole', 'col')), parts along dimension 0
There are 2 independent parts, one for each index of `pole`. A program takes and returns all parts, laid end to end along the dimension named above; an argument that names none is the same for every part. Nothing has to cross between parts.
Inputs may be any that keep to these rules, and one draw needn't show every extreme that they name: `anc_inverse`: symmetric. `parent_pivinv`: symmetric. `parent_mask`: 1 marks a structurally nonzero block of 256 rows. `leaf_mask`: 1 marks a structurally nonzero block of 256 rows.
All inputs are finite; a program needn't handle non-finite values.
Results may differ from a plain program's by a relative error of at most 0.0095.
Values may be sent and summed in bfloat16 or wider, within the bound.
No kernel may reach another device: no remote copies, remote signals or barrier semaphores. Data moves between devices by JAX's collectives and lax.ppermute only.
A program may use at most 64 MiB of HBM per device.

v0:
```python
import jax
import jax.numpy as jnp
from jax import lax
from jax.sharding import PartitionSpec as P

BLOCK = 256
ORDER = 1024


def local(
    anc_inverse,
    parent_pivinv,
    parent_lower,
    parent_mask,
    leaf_lower_par,
    leaf_lower_anc,
    leaf_mask,
    leaf_pivots,
):
    row_index = lax.axis_index("row")
    row_devices = lax.axis_size("row")
    col_index = lax.axis_index("col")
    anc_rows = anc_inverse.shape[0]
    order_rows = parent_pivinv.shape[0]
    col_width = leaf_pivots.shape[0]
    parent_gate = lax.dynamic_slice_in_dim(
        jnp.repeat(parent_mask, BLOCK), row_index * anc_rows, anc_rows
    )
    lower_one = parent_lower * parent_gate[:, None].astype(jnp.bfloat16)
    lower_half = lax.dynamic_slice_in_dim(lower_one, col_index * col_width, col_width, 1)
    leaf_gate = jnp.repeat(leaf_mask, BLOCK)
    gate_par = lax.dynamic_slice_in_dim(leaf_gate[:ORDER], row_index * order_rows, order_rows)
    gate_anc = lax.dynamic_slice_in_dim(leaf_gate[ORDER:], row_index * anc_rows, anc_rows)
    leaf_local = jnp.concatenate(
        [
            leaf_lower_par * gate_par[:, None].astype(jnp.bfloat16),
            leaf_lower_anc * gate_anc[:, None].astype(jnp.bfloat16),
        ],
        axis=0,
    )
    leaf_half = lax.dynamic_slice_in_dim(leaf_local, col_index * col_width, col_width, 1)
    columns = anc_inverse
    product = jnp.dot(
        columns,
        lax.all_gather(lower_half, "row", axis=0, tiled=True),
        preferred_element_type=jnp.float32,
    )
    parent_offdiag = (-product).astype(jnp.bfloat16)
    offdiag_rows = lax.all_gather(parent_offdiag, "col", axis=1, tiled=True)
    columns = lower_one
    diag_sums = lax.psum_scatter(
        lax.dot_general(
            columns, offdiag_rows, (((0,), (0,)), ((), ())), preferred_element_type=jnp.float32
        ),
        "row",
        scatter_dimension=0,
        tiled=True,
    )
    parent_block = parent_pivinv - diag_sums
    parent_round = parent_block.astype(jnp.bfloat16)
    mirrored = lax.all_to_all(offdiag_rows, "row", split_axis=1, concat_axis=0, tiled=True).T
    upper_rows = jnp.concatenate(
        [
            parent_round.reshape(order_rows, row_devices, order_rows),
            mirrored.reshape(order_rows, row_devices, anc_rows),
        ],
        axis=2,
    )
    lower_rows = jnp.concatenate(
        [
            offdiag_rows.reshape(anc_rows, row_devices, order_rows),
            anc_inverse.reshape(anc_rows, row_devices, anc_rows),
        ],
        axis=2,
    )
    inverse_rows = jnp.concatenate(
        [upper_rows.reshape(order_rows, -1), lower_rows.reshape(anc_rows, -1)], axis=0
    )
    columns = inverse_rows
    leaf_product = jnp.dot(
        columns,
        lax.all_gather(leaf_half, "row", axis=0, tiled=True),
        preferred_element_type=jnp.float32,
    )
    leaf_result = (-leaf_product).astype(jnp.bfloat16)
    partial_sums = jnp.sum(leaf_half.astype(jnp.float32) * leaf_result.astype(jnp.float32), axis=0)
    density = leaf_pivots - lax.psum(partial_sums, "row")
    return (
        parent_block,
        parent_offdiag,
        leaf_result[:order_rows],
        leaf_result[order_rows:],
        density,
    )


def solution(mesh):
    placed = (
        P(("pole", "row"), None),
        P(("pole", "row"), None),
        P(("pole", "row"), None),
        P(),
        P(("pole", "row"), None),
        P(("pole", "row"), None),
        P(),
        P(("pole", "col")),
    )
    return jax.shard_map(
        local,
        mesh=mesh,
        in_specs=placed,
        out_specs=(
            P(("pole", "row"), None),
            P(("pole", "row"), "col"),
            P(("pole", "row"), "col"),
            P(("pole", "row"), "col"),
            P(("pole", "col")),
        ),
        check_vma=False,
    )
```

profile of v0, /device:TPU:0, one launch (start us, length us, event | category | flops | bytes accessed | tf_op | source)
XLA Modules:
  0.0 232.6 jit_solution(13250326127232926921)
XLA Ops:
  7.2 0.0 copy-start
  7.2 0.0 all-gather.3.cloned.1.call-start
  7.2 0.6 copy-done
  7.8 0.1 broadcast_bitcast_fusion.2
  7.9 0.1 dynamic-slice_convert_fusion.2
  8.0 1.0 broadcast_multiply_fusion.2
  9.0 0.7 constant_dynamic-slice_fusion
  9.7 0.0 all-gather.3.cloned.1.call-update
  9.7 0.0 reduce-scatter.2.cloned.1.call-start
  9.8 43.8 %all-gather.3.cloned.1.call-done = bf16[1024,512]{1,0:T(8,128)(2,1)} async-done(((bf16[128,512]{1,0:T(8,128)(2,1)}), bf16[1024,512]{1,0:T(8,128)(2,1)}) %all-gather.3.cloned.1.call-update) | async-done | bytes 1048592 | tf_op jit(solution)/shard_map/all_gather | solution.py:45
  53.6 1.7 fusion.2
  55.3 2.0 all_gather.10
  57.3 2.7 %fusion.10 = f32[1024,1024]{1,0:T(8,128)} fusion(bf16[128,1024]{1,0:T(8,128)(2,1)S(1)} %broadcast_multiply_fusion.2, bf16[128,1024]{0,1:T(8,128)(2,1)S(1)} %all_gather.10), kind=kOutput, calls=%fused_computation.28 | convolution fusion | flops 268435456 | bytes 4718592 | tf_op jit(solution)/shard_map/dot_general | solution.py:52
  60.0 0.0 reduce-scatter.2.cloned.1.call-update
  60.1 0.0 copy-start.1
  60.1 0.0 all-gather.5.cloned.1.call-start
  60.1 0.6 copy-done.7
  60.7 0.1 fusion.9
  60.8 0.1 broadcast_bitcast_fusion.1
  60.8 0.1 broadcast_bitcast_fusion
  60.9 0.1 dynamic-slice_convert_fusion
  61.0 0.0 copy-done.4
  61.0 0.1 broadcast_multiply_fusion
  61.1 0.0 copy-done.5
  61.1 0.1 broadcast_multiply_fusion.1
  61.2 0.0 copy-start.3
  61.2 0.7 fusion.6
  62.0 0.0 all-gather.5.cloned.1.call-update
  62.0 0.9 copy.16
  62.8 3.4 %all-to-all-start = ((bf16[128,8,128]{2,0,1:T(8,128)(2,1)}), bf16[128,8,128]{2,0,1:T(8,128)(2,1)S(1)}, u32[]{:S(2)}, u32[]{:S(2)}) async-start(bf16[128,8,128]{2,0,1:T(8,128)(2,1)} %copy.16), calls=%async_computation.1 | async-start | bytes 524288 | tf_op jit(solution)/shard_map/all_to_all | solution.py:61
  66.3 0.0 copy-done.1
  66.3 0.2 copy.22
  66.4 0.8 copy.20
  67.3 15.4 %all-to-all-done = bf16[128,8,128]{2,0,1:T(8,128)(2,1)S(1)} async-done(((bf16[128,8,128]{2,0,1:T(8,128)(2,1)}), bf16[128,8,128]{2,0,1:T(8,128)(2,1)S(1)}, u32[]{:S(2)}, u32[]{:S(2)}) %all-to-all-start) | async-done | bytes 262176 | tf_op jit(solution)/shard_map/all_to_all | solution.py:61
  82.7 0.2 copy.17
  82.9 0.0 copy-start.2
  82.9 69.2 %reduce-scatter.2.cloned.1.call-done = f32[128,1024]{1,0:T(8,128)} async-done(((f32[1024,1024]{1,0:T(8,128)}), f32[128,1024]{1,0:T(8,128)}) %reduce-scatter.2.cloned.1.call-update) | async-done | bytes 524304 | tf_op jit(solution)/shard_map/reduce_scatter | solution.py:51
  152.1 0.0 copy-done.3
  152.1 2.0 convert_bitcast_fusion
  154.1 0.1 pad_maximum_fusion
  154.2 0.4 copy.21
  154.6 48.9 %all-gather.5.cloned.1.call-done = bf16[2048,512]{1,0:T(8,128)(2,1)} async-done(((bf16[256,512]{1,0:T(8,128)(2,1)}), bf16[2048,512]{1,0:T(8,128)(2,1)}) %all-gather.5.cloned.1.call-update) | async-done | bytes 2097168 | tf_op jit(solution)/shard_map/all_gather | solution.py:82
  203.5 0.0 copy-done.2
  203.5 2.4 %multiply_reduce_fusion = (f32[512]{0:T(512)S(1)}, bf16[256,512]{1,0:T(8,128)(2,1)S(1)}) fusion(bf16[256,512]{1,0:T(8,128)(2,1)S(1)} %copy-done.2, bf16[2048,512]{1,0:T(8,128)(2,1)} %all-gather.5.cloned.1.call-done, bf16[128,2048]{0,1:T(8,128)(2,1)S(1)} %bitcast.35, bf16[128,2048]{0,1:T(8,128)(2,1)S(1)} %bitcast.36), kind=kOutput, calls=%fused_computation.12 | convolution fusion | flops 539753984 | bytes 3672064 | tf_op jit(solution)/shard_map/dot_general | solution.py:80
  205.9 0.7 fusion.8
  206.6 18.9 %psum.7 = f32[512]{0:T(512)S(1)} all-reduce(f32[512]{0:T(512)S(1)} %get-tuple-element.21), channel_id=1, replica_groups=mesh['pole'=2,'row'=8,'col'=2] {'row'}, use_global_device_ids=true, to_apply=%region_2.0 | all-reduce | flops 512 | bytes 4096 | tf_op jit(solution)/shard_map/psum | solution.py:87
  225.5 0.0 copy-done.6
  225.5 0.6 sub.7
  (9 shorter events, 0.1 us)
Async XLA Ops:
  7.2 0.7 copy-start
  7.2 46.4 %all-gather.3.cloned.1.call-start = ((), (), s32[]{:S(2)}) async-start(), calls=%async_computation.2 | async-start | bytes 1179648 | tf_op jit(solution)/shard_map/all_gather | solution.py:45
  9.7 142.3 %reduce-scatter.2.cloned.1.call-start = ((), (), s32[]{:S(2)}) async-start(), calls=%async_computation.3 | async-start | bytes 4718592 | tf_op jit(solution)/shard_map/reduce_scatter | solution.py:51
  60.0 0.7 copy-start.7
  60.0 1.0 copy-start.4
  60.0 1.1 copy-start.5
  60.1 6.2 %copy-start.1 = (bf16[128,1024]{1,0:T(8,128)(2,1)S(1)}, bf16[128,1024]{1,0:T(8,128)(2,1)}, u32[]{:S(2)}) copy-start(bf16[128,1024]{1,0:T(8,128)(2,1)} %param.8) | copy-start | bytes 786436
  60.1 143.4 %all-gather.5.cloned.1.call-start = ((), (), s32[]{:S(2)}) async-start(), calls=%async_computation.4 | async-start | bytes 2359296 | tf_op jit(solution)/shard_map/all_gather | solution.py:82
  61.2 90.9 %copy-start.3 = (f32[128,1024]{1,0:T(8,128)S(1)}, f32[128,1024]{1,0:T(8,128)}, u32[]{:S(2)}) copy-start(f32[128,1024]{1,0:T(8,128)} %param.9) | copy-start | bytes 1572868
  62.8 19.9 %all-to-all-start = ((bf16[128,8,128]{2,0,1:T(8,128)(2,1)}), bf16[128,8,128]{2,0,1:T(8,128)(2,1)S(1)}, u32[]{:S(2)}, u32[]{:S(2)}) async-start(bf16[128,8,128]{2,0,1:T(8,128)(2,1)} %copy.16), calls=%async_computation.1 | async-start | bytes 524288 | tf_op jit(solution)/shard_map/all_to_all | solution.py:61
  82.9 120.6 %copy-start.2 = (bf16[256,512]{1,0:T(8,128)(2,1)S(1)}, bf16[256,512]{1,0:T(8,128)(2,1)}, u32[]{:S(2)}) copy-start(bf16[256,512]{1,0:T(8,128)(2,1)} %fusion.6) | copy-start | bytes 786436
  203.5 22.0 %copy-start.6 = (f32[512]{0:T(512)S(1)}, f32[512]{0:T(512)}, u32[]{:S(2)}) copy-start(f32[512]{0:T(512)} %param.15) | copy-start | bytes 6148
Sparse Core Ops, SparseCore 0:
  10.7 42.8 all-gather.2
  60.2 91.8 reduce-scatter.1
  154.4 49.0 all-gather.4
where the time goes:
time: 233 us
  waiting for transfers between devices  177 us (76%)
  blocking collectives  20.9 us (9%)
  between operations  13.9 us (6%)
  matrix products  6.8 us (3%)
  local copies, waits for them, and re-layouts  5.36 us (2%)
  other arithmetic  4.75 us (2%)
  starting transfers between devices  3.53 us (2%)
    reduce_scatter x1, waiting for transfers between devices, local(): lax.psum_scatter(lax.dot_general(columns, offdiag_rows, (((0,), (0,)), ((...  69.2 us
    all_gather x1, waiting for transfers between devices, local(): lax.all_gather(leaf_half, 'row', axis=0, tiled=True)  48.9 us
    all_gather x1, waiting for transfers between devices, local(): lax.all_gather(lower_half, 'row', axis=0, tiled=True)  43.8 us
    psum x1, blocking collectives, local(): density = leaf_pivots - lax.psum(partial_sums, 'row')  18.9 us
    all_to_all x1, waiting for transfers between devices, local(): lax.all_to_all(offdiag_rows, 'row', split_axis=1, concat_axis=0, tiled=True)  15.4 us
  transfers between devices with their start and end apart: 4, of which 4 were waited for; matrix products, arithmetic and copies ran while one was open for 2% of the time, Pallas kernels for 0%

commit v1 on v0

--- a/solution.py
+++ b/solution.py
@@ -5,6 +5,28 @@
 
 BLOCK = 256
 ORDER = 1024
+
+
+def joined_along(blocks, dim):
+    shape = list(blocks.shape[1:])
+    shape[dim] *= blocks.shape[0]
+    return jnp.moveaxis(blocks, 0, dim).reshape(shape)
+
+
+def ring_gather(x, axis, dim):
+    count = lax.axis_size(axis)
+    pairs = [(i, (i + 1) % count) for i in range(count)]
+    back = [(b, a) for a, b in pairs]
+    lower, upper = ([], [])
+    for hop in range(count - 1):
+        if hop % 2 == 0:
+            lower.append(lax.ppermute(lower[-1] if lower else x, axis, pairs))
+        else:
+            upper.append(lax.ppermute(upper[-1] if upper else x, axis, back))
+    pieces = jnp.stack([*lower[::-1], x, *upper])
+    shift = lax.axis_index(axis) - len(lower)
+    pieces = pieces[(jnp.arange(count) - shift) % count]
+    return joined_along(pieces, dim)
 
 
 def local(
@@ -78,9 +100,7 @@
     )
     columns = inverse_rows
     leaf_product = jnp.dot(
-        columns,
-        lax.all_gather(leaf_half, "row", axis=0, tiled=True),
-        preferred_element_type=jnp.float32,
+        columns, ring_gather(leaf_half, "row", 0), preferred_element_type=jnp.float32
     )
     leaf_result = (-leaf_product).astype(jnp.bfloat16)
     partial_sums = jnp.sum(leaf_half.astype(jnp.float32) * leaf_result.astype(jnp.float32), axis=0)

time: 233 us -> 202 us (0.87)
  waiting for transfers between devices: 177 us -> 118 us
  starting transfers between devices: 3.53 us -> 23 us
  local copies, waits for them, and re-layouts: 5.36 us -> 13.2 us
    all_gather x1 -> x0, waiting for transfers between devices: 48.9 us -> none  [local(): lax.all_gather(leaf_half, 'row', axis=0, tiled=True)]
    ppermute x0 -> x7, waiting for transfers between devices: none -> 46.9 us  [the longest x4 46.8 us: ring_gather(): lower.append(lax.ppermute(lower[-1] if lower else x, axis, pairs))]
    reduce_scatter x1, waiting for transfers between devices: 69.2 us -> 24.7 us  [local(): lax.psum_scatter(lax.dot_general(columns, offdiag_rows, (((0,), (0,)), ((...]
    ppermute x0 -> x7, starting transfers between devices: none -> 14.7 us  [the longest x3 14 us: ring_gather(): upper.append(lax.ppermute(upper[-1] if upper else x, axis, back))]
    all_to_all x1, waiting for transfers between devices: 15.4 us -> 2.65 us  [local(): lax.all_to_all(offdiag_rows, 'row', split_axis=1, concat_axis=0, tiled=True)]
    all_to_all x1, starting transfers between devices: 3.41 us -> 8.19 us  [local(): lax.all_to_all(offdiag_rows, 'row', split_axis=1, concat_axis=0, tiled=True)]
    unnamed x24 -> x39, local copies, waits for them, and re-layouts: 2.25 us -> 6.28 us
  transfers between devices with their start and end apart: 4 -> 10, of which waited for: 4 -> 8; matrix products, arithmetic and copies ran while one was open for 2% -> 5% of each run, Pallas kernels for 0% -> 0%
where the time goes in v1:
time: 202 us
  waiting for transfers between devices  118 us (58%)
  starting transfers between devices  23 us (11%)
  blocking collectives  22.2 us (11%)
  between operations  14.2 us (7%)
  local copies, waits for them, and re-layouts  13.2 us (7%)
  matrix products  6.39 us (3%)
  other arithmetic  4.85 us (2%)
    ppermute x4, waiting for transfers between devices, ring_gather(): lower.append(lax.ppermute(lower[-1] if lower else x, axis, pairs))  46.8 us
    all_gather x1, waiting for transfers between devices, local(): lax.all_gather(lower_half, 'row', axis=0, tiled=True)  43.8 us
    reduce_scatter x1, waiting for transfers between devices, local(): lax.psum_scatter(lax.dot_general(columns, offdiag_rows, (((0,), (0,)), ((...  24.7 us
    psum x1, blocking collectives, local(): density = leaf_pivots - lax.psum(partial_sums, 'row')  20.2 us
    ppermute x3, starting transfers between devices, ring_gather(): upper.append(lax.ppermute(upper[-1] if upper else x, axis, back))  14 us
    all_to_all x1, starting transfers between devices, local(): lax.all_to_all(offdiag_rows, 'row', split_axis=1, concat_axis=0, tiled=True)  8.19 us
    unnamed x39, local copies, waits for them, and re-layouts  6.28 us
  transfers between devices with their start and end apart: 10, of which 8 were waited for; matrix products, arithmetic and copies ran while one was open for 5% of the time, Pallas kernels for 0%

profile of v1, /device:TPU:0, one launch (start us, length us, event | category | flops | bytes accessed | tf_op | source)
XLA Modules:
  0.0 201.9 jit_solution(11765824256758524244)
XLA Ops:
  7.2 0.6 copy-done
  7.8 0.1 broadcast_bitcast_fusion.2
  7.9 0.1 dynamic-slice_convert_fusion.2
  8.0 1.0 broadcast_multiply_fusion.2
  9.0 0.7 constant_dynamic-slice_fusion
  9.7 0.0 reduce-scatter.2.cloned.1.call-start
  9.8 43.8 %all-gather.2.cloned.1.call-done = bf16[1024,512]{1,0:T(8,128)(2,1)} async-done(((bf16[128,512]{1,0:T(8,128)(2,1)}), bf16[1024,512]{1,0:T(8,128)(2,1)}) %all-gather.2.cloned.1.call-update) | async-done | bytes 1048592 | tf_op jit(solution)/shard_map/all_gather | solution.py:67
  53.6 1.7 fusion.2
  55.3 2.0 all_gather.7
  57.3 2.7 %fusion.12 = f32[1024,1024]{1,0:T(8,128)} fusion(bf16[128,1024]{1,0:T(8,128)(2,1)S(1)} %broadcast_multiply_fusion.2, bf16[128,1024]{0,1:T(8,128)(2,1)S(1)} %all_gather.7), kind=kOutput, calls=%fused_computation.44 | convolution fusion | flops 268435456 | bytes 4718592 | tf_op jit(solution)/shard_map/dot_general | solution.py:74
  60.0 0.6 copy-done.11
  60.7 0.1 fusion.11
  60.7 0.1 broadcast_bitcast_fusion
  60.8 0.1 broadcast_bitcast_fusion.1
  60.9 0.1 dynamic-slice_convert_fusion
  61.0 0.1 broadcast_multiply_fusion.1
  61.1 0.1 broadcast_multiply_fusion
  61.2 0.6 collective-permute-start
  61.8 12.7 %collective-permute-done = bf16[256,512]{1,0:T(8,128)(2,1)S(1)} collective-permute-done((bf16[256,512]{1,0:T(8,128)(2,1)S(1)}, bf16[256,512]{1,0:T(8,128)(2,1)S(1)}, u32[]{:S(2)}, u32[]{:S(2)}) %collective-permute-start) | collective-permute-done | bytes 262176 | tf_op jit(solution)/shard_map/ppermute | solution.py:23
  74.5 4.7 %collective-permute-start.4 = (bf16[256,512]{1,0:T(8,128)(2,1)S(1)}, bf16[256,512]{1,0:T(8,128)(2,1)S(1)}, u32[]{:S(2)}, u32[]{:S(2)}) collective-permute-start(bf16[256,512]{1,0:T(8,128)(2,1)S(1)} %fusion.6), channel_id=1, source_target_pairs={{2,0},{4,2},{6,4},{8,6},{10,8},{12,10},{14,12},{0,14},{3,1},{5,3},... | collective-permute-start | bytes 786440 | tf_op jit(solution)/shard_map/ppermute | solution.py:25
  79.2 11.8 %collective-permute-done.1 = bf16[256,512]{1,0:T(8,128)(2,1)S(1)} collective-permute-done((bf16[256,512]{1,0:T(8,128)(2,1)S(1)}, bf16[256,512]{1,0:T(8,128)(2,1)S(1)}, u32[]{:S(2)}, u32[]{:S(2)}) %collective-permute-start.1) | collective-permute-done | bytes 262176 | tf_op jit(solution)/shard_map/ppermute | solution.py:23
  91.1 4.7 %collective-permute-start.5 = (bf16[256,512]{1,0:T(8,128)(2,1)S(1)}, bf16[256,512]{1,0:T(8,128)(2,1)}, u32[]{:S(2)}, u32[]{:S(2)}) collective-permute-start(bf16[256,512]{1,0:T(8,128)(2,1)S(1)} %collective-permute-done.4), channel_id=1, source_target_pairs={{2,0},{4,2},{6,4},{8,6},{10,8},{12,10},{14,12},{0,14},{3,1},{5,3},... | collective-permute-start | bytes 786440 | tf_op jit(solution)/shard_map/ppermute | solution.py:25
  95.8 11.4 %collective-permute-done.2 = bf16[256,512]{1,0:T(8,128)(2,1)S(1)} collective-permute-done((bf16[256,512]{1,0:T(8,128)(2,1)S(1)}, bf16[256,512]{1,0:T(8,128)(2,1)S(1)}, u32[]{:S(2)}, u32[]{:S(2)}) %collective-permute-start.2) | collective-permute-done | bytes 262176 | tf_op jit(solution)/shard_map/ppermute | solution.py:23
  107.2 0.0 collective-permute-start.3
  107.2 0.2 copy.22
  107.4 0.1 collective-permute-done.5
  107.6 4.6 %collective-permute-start.6 = (bf16[256,512]{1,0:T(8,128)(2,1)}, bf16[256,512]{1,0:T(8,128)(2,1)}, u32[]{:S(2)}, u32[]{:S(2)}) collective-permute-start(bf16[256,512]{1,0:T(8,128)(2,1)} %collective-permute-done.5), channel_id=1, source_target_pairs={{2,0},{4,2},{6,4},{8,6},{10,8},{12,10},{14,12},{0,14},{3,1},{5,3},... | collective-permute-start | bytes 786440 | tf_op jit(solution)/shard_map/ppermute | solution.py:25
  112.2 10.9 %collective-permute-done.3 = bf16[256,512]{1,0:T(8,128)(2,1)} collective-permute-done((bf16[256,512]{1,0:T(8,128)(2,1)S(1)}, bf16[256,512]{1,0:T(8,128)(2,1)}, u32[]{:S(2)}, u32[]{:S(2)}) %collective-permute-start.3) | collective-permute-done | bytes 262176 | tf_op jit(solution)/shard_map/ppermute | solution.py:23
  123.1 1.0 bitcast_dynamic-update-slice_fusion.7
  124.1 1.0 bitcast_dynamic-update-slice_fusion.6
  125.1 1.0 bitcast_dynamic-update-slice_fusion.5
  126.1 0.9 copy.16
  127.0 8.2 %all-to-all-start = ((bf16[128,8,128]{2,0,1:T(8,128)(2,1)}), bf16[128,8,128]{2,0,1:T(8,128)(2,1)S(1)}, u32[]{:S(2)}, u32[]{:S(2)}) async-start(bf16[128,8,128]{2,0,1:T(8,128)(2,1)} %copy.16), calls=%async_computation.1 | async-start | bytes 524288 | tf_op jit(solution)/shard_map/all_to_all | solution.py:83
  135.2 1.0 bitcast_dynamic-update-slice_fusion.1
  136.2 1.0 bitcast_dynamic-update-slice_fusion
  137.1 2.0 %gather_fusion = bf16[8,256,512]{2,1,0:T(8,128)(2,1)} fusion(bf16[8,256,512]{2,1,0:T(8,128)(2,1)S(1)} %bitcast_dynamic-update-slice_fusion, s32[1024]{0:T(1024)S(1)} %pad_clamp_fusion), kind=kCustom, calls=%fused_computation | custom fusion | bytes 4194336 | tf_op jit(solution)/shard_map/gather | solution.py:28
  139.2 0.8 copy.20
  139.9 0.8 pad_maximum_fusion.1
  140.7 2.6 %all-to-all-done = bf16[128,8,128]{2,0,1:T(8,128)(2,1)S(1)} async-done(((bf16[128,8,128]{2,0,1:T(8,128)(2,1)}), bf16[128,8,128]{2,0,1:T(8,128)(2,1)S(1)}, u32[]{:S(2)}, u32[]{:S(2)}) %all-to-all-start) | async-done | bytes 262176 | tf_op jit(solution)/shard_map/all_to_all | solution.py:83
  143.4 0.2 copy.17
  143.6 24.7 %reduce-scatter.2.cloned.1.call-done = f32[128,1024]{1,0:T(8,128)} async-done(((f32[1024,1024]{1,0:T(8,128)}), f32[128,1024]{1,0:T(8,128)}) %reduce-scatter.2.cloned.1.call-update) | async-done | bytes 524304 | tf_op jit(solution)/shard_map/reduce_scatter | solution.py:73
  168.3 2.0 convert_bitcast_fusion
  170.3 0.1 pad_maximum_fusion
  170.4 1.2 copy.21
  171.6 2.0 multiply_reduce_fusion
  173.6 0.7 fusion.10
  174.3 20.2 %psum.7 = f32[512]{0:T(512)S(1)} all-reduce(f32[512]{0:T(512)S(1)} %get-tuple-element.21), channel_id=1, replica_groups=mesh['pole'=2,'row'=8,'col'=2] {'row'}, use_global_device_ids=true, to_apply=%region_2.3 | all-reduce | flops 512 | bytes 4096 | tf_op jit(solution)/shard_map/psum | solution.py:107
  194.5 0.6 sub.26
  (39 shorter events, 0.3 us)
Async XLA Ops:
  7.2 0.7 copy-start
  7.2 46.4 %all-gather.2.cloned.1.call-start = ((), (), s32[]{:S(2)}) async-start(), calls=%async_computation.2 | async-start | bytes 1179648 | tf_op jit(solution)/shard_map/all_gather | solution.py:67
  9.7 158.6 %reduce-scatter.2.cloned.1.call-start = ((), (), s32[]{:S(2)}) async-start(), calls=%async_computation.3 | async-start | bytes 4718592 | tf_op jit(solution)/shard_map/reduce_scatter | solution.py:73
  60.0 0.7 copy-start.11
  60.0 1.0 copy-start.4
  60.0 1.1 copy-start.5
  60.0 47.2 %copy-start.2 = (bf16[128,1024]{1,0:T(8,128)(2,1)S(1)}, bf16[128,1024]{1,0:T(8,128)(2,1)}, u32[]{:S(2)}) copy-start(bf16[128,1024]{1,0:T(8,128)(2,1)} %param.8) | copy-start | bytes 786436
  61.2 13.3 %collective-permute-start = (bf16[256,512]{1,0:T(8,128)(2,1)S(1)}, bf16[256,512]{1,0:T(8,128)(2,1)S(1)}, u32[]{:S(2)}, u32[]{:S(2)}) collective-permute-start(bf16[256,512]{1,0:T(8,128)(2,1)S(1)} %fusion.6), channel_id=1, source_target_pairs={{0,2},{2,4},{4,6},{6,8},{8,10},{10,12},{12,14},{14,0},{1,3},{3,5},... | collective-permute-start | bytes 786440 | tf_op jit(solution)/shard_map/ppermute | solution.py:23
  74.5 16.5 %collective-permute-start.1 = (bf16[256,512]{1,0:T(8,128)(2,1)S(1)}, bf16[256,512]{1,0:T(8,128)(2,1)S(1)}, u32[]{:S(2)}, u32[]{:S(2)}) collective-permute-start(bf16[256,512]{1,0:T(8,128)(2,1)S(1)} %collective-permute-done), channel_id=1, source_target_pairs={{0,2},{2,4},{4,6},{6,8},{8,10},{10,12},{12,14},{14,0},{1,3},{3,5},... | collective-permute-start | bytes 786440 | tf_op jit(solution)/shard_map/ppermute | solution.py:23
  74.5 16.5 %collective-permute-start.4 = (bf16[256,512]{1,0:T(8,128)(2,1)S(1)}, bf16[256,512]{1,0:T(8,128)(2,1)S(1)}, u32[]{:S(2)}, u32[]{:S(2)}) collective-permute-start(bf16[256,512]{1,0:T(8,128)(2,1)S(1)} %fusion.6), channel_id=1, source_target_pairs={{2,0},{4,2},{6,4},{8,6},{10,8},{12,10},{14,12},{0,14},{3,1},{5,3},... | collective-permute-start | bytes 786440 | tf_op jit(solution)/shard_map/ppermute | solution.py:25
  91.1 16.1 %copy-start.8 = (bf16[256,512]{1,0:T(8,128)(2,1)}, bf16[256,512]{1,0:T(8,128)(2,1)S(1)}, u32[]{:S(2)}) copy-start(bf16[256,512]{1,0:T(8,128)(2,1)S(1)} %collective-permute-done.1) | copy-start | bytes 786436
  91.1 16.1 %collective-permute-start.2 = (bf16[256,512]{1,0:T(8,128)(2,1)S(1)}, bf16[256,512]{1,0:T(8,128)(2,1)S(1)}, u32[]{:S(2)}, u32[]{:S(2)}) collective-permute-start(bf16[256,512]{1,0:T(8,128)(2,1)S(1)} %collective-permute-done.1), channel_id=1, source_target_pairs={{0,2},{2,4},{4,6},{6,8},{8,10},{10,12},{12,14},{14,0},{1,3},{3,5},... | collective-permute-start | bytes 786440 | tf_op jit(solution)/shard_map/ppermute | solution.py:23
  91.1 21.1 %copy-start.6 = (bf16[256,512]{1,0:T(8,128)(2,1)}, bf16[256,512]{1,0:T(8,128)(2,1)S(1)}, u32[]{:S(2)}) copy-start(bf16[256,512]{1,0:T(8,128)(2,1)S(1)} %collective-permute-done.4) | copy-start | bytes 786436
  91.1 16.5 %collective-permute-start.5 = (bf16[256,512]{1,0:T(8,128)(2,1)S(1)}, bf16[256,512]{1,0:T(8,128)(2,1)}, u32[]{:S(2)}, u32[]{:S(2)}) collective-permute-start(bf16[256,512]{1,0:T(8,128)(2,1)S(1)} %collective-permute-done.4), channel_id=1, source_target_pairs={{2,0},{4,2},{6,4},{8,6},{10,8},{12,10},{14,12},{0,14},{3,1},{5,3},... | collective-permute-start | bytes 786440 | tf_op jit(solution)/shard_map/ppermute | solution.py:25
  107.2 5.0 %copy-start.9 = (bf16[256,512]{1,0:T(8,128)(2,1)}, bf16[256,512]{1,0:T(8,128)(2,1)S(1)}, u32[]{:S(2)}) copy-start(bf16[256,512]{1,0:T(8,128)(2,1)S(1)} %collective-permute-done.2) | copy-start | bytes 786436
  107.2 15.9 %collective-permute-start.3 = (bf16[256,512]{1,0:T(8,128)(2,1)S(1)}, bf16[256,512]{1,0:T(8,128)(2,1)}, u32[]{:S(2)}, u32[]{:S(2)}) collective-permute-start(bf16[256,512]{1,0:T(8,128)(2,1)S(1)} %collective-permute-done.2), channel_id=1, source_target_pairs={{0,2},{2,4},{4,6},{6,8},{8,10},{10,12},{12,14},{14,0},{1,3},{3,5},... | collective-permute-start | bytes 786440 | tf_op jit(solution)/shard_map/ppermute | solution.py:23
  107.6 28.6 %collective-permute-start.6 = (bf16[256,512]{1,0:T(8,128)(2,1)}, bf16[256,512]{1,0:T(8,128)(2,1)}, u32[]{:S(2)}, u32[]{:S(2)}) collective-permute-start(bf16[256,512]{1,0:T(8,128)(2,1)} %collective-permute-done.5), channel_id=1, source_target_pairs={{2,0},{4,2},{6,4},{8,6},{10,8},{12,10},{14,12},{0,14},{3,1},{5,3},... | collective-permute-start | bytes 786440 | tf_op jit(solution)/shard_map/ppermute | solution.py:25
  123.1 3.0 %copy-start.7 = (bf16[256,512]{1,0:T(8,128)(2,1)S(1)}, bf16[256,512]{1,0:T(8,128)(2,1)}, u32[]{:S(2)}) copy-start(bf16[256,512]{1,0:T(8,128)(2,1)} %copy-done.6) | copy-start | bytes 786436
  127.0 16.4 %all-to-all-start = ((bf16[128,8,128]{2,0,1:T(8,128)(2,1)}), bf16[128,8,128]{2,0,1:T(8,128)(2,1)S(1)}, u32[]{:S(2)}, u32[]{:S(2)}) async-start(bf16[128,8,128]{2,0,1:T(8,128)(2,1)} %copy.16), calls=%async_computation.1 | async-start | bytes 524288 | tf_op jit(solution)/shard_map/all_to_all | solution.py:83
  139.2 29.1 %copy-start.3 = (f32[128,1024]{1,0:T(8,128)S(1)}, f32[128,1024]{1,0:T(8,128)}, u32[]{:S(2)}) copy-start(f32[128,1024]{1,0:T(8,128)} %param.9) | copy-start | bytes 1572868
  143.6 28.0 %copy-start.1 = (bf16[8,256,512]{2,1,0:T(8,128)(2,1)S(1)}, bf16[8,256,512]{2,1,0:T(8,128)(2,1)}, u32[]{:S(2)}) copy-start(bf16[8,256,512]{2,1,0:T(8,128)(2,1)} %gather_fusion) | copy-start | bytes 6291460
  171.6 22.9 %copy-start.10 = (f32[512]{0:T(512)S(1)}, f32[512]{0:T(512)}, u32[]{:S(2)}) copy-start(f32[512]{0:T(512)} %param.15) | copy-start | bytes 6148
Sparse Core Ops, SparseCore 0:
  10.7 42.8 all-gather.1
  60.2 108.0 reduce-scatter.1
